TPU v7x, 512 devices: a whole 4x8x8 slice. The times are simulated.
512 devices in a mesh: seq: 32 (over x, y), head: 8 (over z), doc: 2 (over core).
Axes of the slice: x: 4, y: 8, z: 8, core: 2. Of those that a mesh axis runs over, the one named last changes fastest.
Arguments:
- byte_states: bfloat16 [32768, 1024], P(('doc', 'seq')), parts along dimension 0, may hold values from -36 to 36
- conv_kernel: float32 [4, 1024], replicated, may hold values from -3 to 3
- mix_weight: bfloat16 [1024, 1024], replicated, may hold values from -0.1875 to 0.1875
- norm_gain: float32 [1024], replicated, may hold values from 0.1 to 1.9
- query_weight: bfloat16 [1024, 1024], P(None, 'head'), may hold values from -3 to 3
- key_weight: bfloat16 [1024, 1024], P(None, 'head'), may hold values from -3 to 3
- value_weight: bfloat16 [1024, 1024], P(None, 'head'), may hold values from -0.1875 to 0.1875
- boundaries: int32 [4096], P(('doc', 'seq')), parts along dimension 0, may hold values from 0 to 511, as said below
- span_counts: int32 [64], P(('doc', 'seq')), parts along dimension 0, may hold values from 16 to 64, as said below
- grad_attended: bfloat16 [4096, 1024], P(('doc', 'seq'), 'head'), parts along dimension 0, may hold values from -6 to 6
Outputs:
- attended: bfloat16 [4096, 1024], P(('doc', 'seq'), 'head'), parts along dimension 0
- grad_bytes: bfloat16 [32768, 1024], P(('doc', 'seq')), parts along dimension 0
There are 2 independent parts, one for each index of `doc`. A program takes and returns all parts, laid end to end along the dimension named above; an argument that names none is the same for every part. Nothing has to cross between parts.
Inputs may be any that keep to these rules, and one draw needn't show every extreme that they name: `span_counts`: number of spans starting in each shard; in every draw some shard has exactly 64. `boundaries`: in each shard's 64 slots the first span_counts entries are strictly increasing byte positions inside the shard, the first of them 0; the remaining slots hold 0.
All inputs are finite; a program needn't handle non-finite values.
Results may differ from a plain program's by a relative error of at most 0.017.
Values may be sent and summed in bfloat16 or wider, within the bound.
No kernel may reach another device: no remote copies, remote signals or barrier semaphores. Data moves between devices by JAX's collectives and lax.ppermute only.
A program may use at most 64 MiB of HBM per device.

v0:
```python
import math
import jax
import jax.numpy as jnp
from jax import lax
from jax.sharding import PartitionSpec as P

D = 1024
HD = 128
KCONV = 4
masked_score = -1e30


def passed_along(array, axis, by):
    devices = lax.axis_size(axis)
    pairs = [(i, i + by) for i in range(devices) if 0 <= i + by < devices]
    return lax.ppermute(array, axis, pairs)


def neighbour(rim_rows, offset_by):
    return passed_along(rim_rows, "seq", offset_by)


def per_device(
    byte_states,
    conv_kernel,
    mix_weight,
    norm_gain,
    query_weight,
    key_weight,
    value_weight,
    boundaries,
    span_counts,
    grad_attended,
):
    row_count = byte_states.shape[0]
    slot_count = boundaries.shape[0]
    head_width = query_weight.shape[1]
    local_heads = head_width // HD
    score_scale = 1.0 / math.sqrt(HD)
    shard_index = lax.axis_index("seq")
    first_slot = shard_index * slot_count
    own_ids = first_slot + jnp.arange(slot_count, dtype=jnp.int32)
    before_rim = neighbour(byte_states[row_count - (KCONV - 1) :].astype(jnp.float32), 1)
    extended = jnp.concatenate([before_rim.astype(jnp.bfloat16), byte_states], axis=0)
    span_depth = conv_kernel[0] * jnp.take(extended, boundaries + (KCONV - 1), axis=0).astype(
        jnp.float32
    )
    for offset in range(1, KCONV):
        tapped = jnp.take(extended, boundaries + (KCONV - 1 - offset), axis=0).astype(jnp.float32)
        span_depth = span_depth + conv_kernel[offset] * tapped
    span_depth = span_depth.astype(jnp.bfloat16)
    span_bytes = jnp.take(byte_states, boundaries, axis=0).astype(jnp.float32)
    live_mask = jnp.arange(slot_count, dtype=jnp.int32) < span_counts[0]
    live_half = live_mask.astype(jnp.bfloat16)
    span_state = span_bytes + jnp.dot(span_depth, mix_weight, preferred_element_type=jnp.float32)
    inverse_rms = lax.rsqrt(jnp.mean(span_state * span_state, axis=1) + 1e-05)
    normed = (span_state * inverse_rms[:, None] * norm_gain).astype(jnp.bfloat16)
    queries = jnp.dot(normed, query_weight, preferred_element_type=jnp.float32).astype(jnp.bfloat16)
    key_rows = jnp.dot(normed, key_weight, preferred_element_type=jnp.float32).astype(jnp.bfloat16)
    value_rows = jnp.dot(normed, value_weight, preferred_element_type=jnp.float32).astype(
        jnp.bfloat16
    )
    grad_rows = jnp.where(live_mask[:, None], grad_attended, jnp.zeros_like(grad_attended))
    query_heads = queries.reshape(slot_count, local_heads, HD)
    key_heads = key_rows.reshape(slot_count, local_heads, HD)
    value_heads = value_rows.reshape(slot_count, local_heads, HD)
    grad_heads = grad_rows.reshape(slot_count, local_heads, HD)
    piece_keys = lax.all_gather(key_rows, "seq", axis=0, tiled=True)
    piece_values = lax.all_gather(value_rows, "seq", axis=0, tiled=True)
    piece_live = lax.all_gather(live_half, "seq", axis=0, tiled=True)
    running_max = jnp.full((local_heads, slot_count), masked_score, jnp.float32)
    piece_rows = piece_keys.shape[0]
    key_ids = jnp.arange(piece_rows, dtype=jnp.int32)
    allowed = (key_ids[None, :] <= own_ids[:, None]) & (piece_live[None, :] > 0.5)
    scores = (
        jnp.einsum(
            "qhd,khd->hqk",
            query_heads,
            piece_keys.reshape(piece_rows, local_heads, HD),
            preferred_element_type=jnp.float32,
        )
        * score_scale
    )
    scores = jnp.where(allowed[None], scores, masked_score)
    new_max = jnp.maximum(running_max, jnp.max(scores, axis=2))
    softmax_part = jnp.exp(scores - new_max[:, :, None])
    new_sum = jnp.sum(softmax_part, axis=2)
    product = jnp.einsum(
        "hqk,khd->hqd",
        softmax_part.astype(jnp.bfloat16),
        piece_values.reshape(piece_rows, local_heads, HD),
        preferred_element_type=jnp.float32,
    )
    attention = jnp.transpose(product / new_sum[:, :, None], (1, 0, 2)).reshape(
        slot_count, head_width
    )
    attended = jnp.where(live_mask[:, None], attention, jnp.float32(0.0)).astype(jnp.bfloat16)
    log_rows = jnp.transpose(new_max + jnp.log(new_sum))
    delta_rows = jnp.sum(
        grad_heads.astype(jnp.float32)
        * attended.reshape(slot_count, local_heads, HD).astype(jnp.float32),
        axis=2,
    )
    own_logs = jnp.transpose(log_rows)
    own_deltas = jnp.transpose(delta_rows)
    all_logs, all_deltas = (
        lax.all_gather(log_rows, "seq", axis=0, tiled=True),
        lax.all_gather(delta_rows, "seq", axis=0, tiled=True),
    )
    piece_queries = lax.all_gather(queries, "seq", axis=0, tiled=True)
    piece_keys = lax.all_gather(key_rows, "seq", axis=0, tiled=True)
    piece_values = lax.all_gather(value_rows, "seq", axis=0, tiled=True)
    piece_grads = lax.all_gather(grad_rows, "seq", axis=0, tiled=True)
    piece_live = lax.all_gather(live_half, "seq", axis=0, tiled=True)
    piece_rows = piece_keys.shape[0]
    key_ids = jnp.arange(piece_rows, dtype=jnp.int32)
    key_part = piece_keys.reshape(piece_rows, local_heads, HD)
    allowed = (key_ids[None, :] <= own_ids[:, None]) & (piece_live[None, :] > 0.5)
    scores = (
        jnp.einsum("qhd,khd->hqk", query_heads, key_part, preferred_element_type=jnp.float32)
        * score_scale
    )
    scores = jnp.where(allowed[None], scores, masked_score)
    probs_full = jnp.exp(scores - own_logs[:, :, None])
    grad_probs = jnp.einsum(
        "qhd,khd->hqk",
        grad_heads,
        piece_values.reshape(piece_rows, local_heads, HD),
        preferred_element_type=jnp.float32,
    )
    grad_scores = (probs_full * (grad_probs - own_deltas[:, :, None])).astype(jnp.bfloat16)
    new_query = jnp.einsum(
        "hqk,khd->hqd", grad_scores, key_part, preferred_element_type=jnp.float32
    )
    piece_rows = piece_queries.shape[0]
    piece_ids = jnp.arange(piece_rows, dtype=jnp.int32)
    query_part = piece_queries.reshape(piece_rows, local_heads, HD)
    grad_part = piece_grads.reshape(piece_rows, local_heads, HD)
    piece_logs = jnp.transpose(all_logs)
    piece_deltas = jnp.transpose(all_deltas)
    allowed = (own_ids[None, :] <= piece_ids[:, None]) & live_mask[None, :]
    scores = (
        jnp.einsum("qhd,khd->hqk", query_part, key_heads, preferred_element_type=jnp.float32)
        * score_scale
    )
    scores = jnp.where(allowed[None], scores, masked_score)
    probs_full = jnp.exp(scores - piece_logs[:, :, None])
    grad_value = jnp.einsum(
        "hqk,qhd->hkd",
        probs_full.astype(jnp.bfloat16),
        grad_part,
        preferred_element_type=jnp.float32,
    )
    grad_probs = jnp.einsum(
        "qhd,khd->hqk", grad_part, value_heads, preferred_element_type=jnp.float32
    )
    grad_scores = (probs_full * (grad_probs - piece_deltas[:, :, None])).astype(jnp.bfloat16)
    grad_key = jnp.einsum(
        "hqk,qhd->hkd", grad_scores, query_part, preferred_element_type=jnp.float32
    )

    def to_rows(stacked):
        return jnp.transpose(stacked, (1, 0, 2)).reshape(slot_count, head_width)

    contract = (((1,), (1,)), ((), ()))
    query_grad_rows = (to_rows(new_query) * score_scale).astype(jnp.bfloat16)
    key_grad_rows = (to_rows(grad_key) * score_scale).astype(jnp.bfloat16)
    value_grad_rows = to_rows(grad_value).astype(jnp.bfloat16)
    partial_normed = lax.dot_general(
        query_grad_rows, query_weight, contract, preferred_element_type=jnp.float32
    )
    partial_normed = partial_normed + lax.dot_general(
        key_grad_rows, key_weight, contract, preferred_element_type=jnp.float32
    )
    partial_normed = partial_normed + lax.dot_general(
        value_grad_rows, value_weight, contract, preferred_element_type=jnp.float32
    )
    grad_normed = lax.psum(partial_normed.astype(jnp.bfloat16), "head").astype(jnp.float32)
    scaled_grad = norm_gain * grad_normed
    cubed = inverse_rms * inverse_rms * inverse_rms
    grad_state = (
        inverse_rms[:, None] * scaled_grad
        - span_state * cubed[:, None] * jnp.mean(scaled_grad * span_state, axis=1)[:, None]
    )
    grad_state = jnp.where(live_mask[:, None], grad_state, jnp.float32(0.0))
    mixed_grad = lax.dot_general(
        grad_state.astype(jnp.bfloat16), mix_weight, contract, preferred_element_type=jnp.float32
    )
    spread_mix = jnp.zeros((row_count, D), jnp.float32).at[boundaries].add(mixed_grad)
    residual_grad = jnp.zeros((row_count, D), jnp.float32).at[boundaries].add(grad_state)
    after_rim = neighbour(spread_mix[: KCONV - 1], -1)
    padded_grad = jnp.concatenate([spread_mix, after_rim], axis=0)
    conv_grad = conv_kernel[0] * spread_mix
    for offset in range(1, KCONV):
        conv_grad = conv_grad + conv_kernel[offset] * padded_grad[offset : offset + row_count]
    grad_bytes = (residual_grad + conv_grad).astype(jnp.bfloat16)
    return (attended, grad_bytes)


def solution(mesh):
    return jax.shard_map(
        per_device,
        mesh=mesh,
        in_specs=(
            P(("doc", "seq"), None),
            P(),
            P(),
            P(),
            P(None, "head"),
            P(None, "head"),
            P(None, "head"),
            P(("doc", "seq")),
            P(("doc", "seq")),
            P(("doc", "seq"), "head"),
        ),
        out_specs=(P(("doc", "seq"), "head"), P(("doc", "seq"), None)),
        check_vma=False,
    )
```

profile of v0, /device:TPU:56, one launch (start us, length us, event | category | flops | bytes accessed | tf_op | source)
XLA Modules:
  0.0 557.7 jit_solution(17123047837741712854)
XLA Ops:
  8.1 2.6 collective-permute-start
  16.0 63.5 %all-reduce = bf16[2048]{0:T(1024)(128)(2,1)S(1)} all-reduce(bf16[2048]{0:T(1024)(128)(2,1)S(1)} %dynamic-update-slice), channel_id=1, replica_groups=mesh['seq'=32,'head'=8,'doc'=2] {'seq'}, use_global_device_ids=true, to_apply=%add | all-reduce | flops 2048 | bytes 8192
  82.1 2.2 gather_fusion
  84.3 1.5 pad_maximum_fusion
  91.2 1.9 multiply_reduce_fusion.1
  93.9 60.8 %all_gather.27 = bf16[2048,128]{1,0:T(8,128)(2,1)} all-gather(bf16[64,128]{1,0:T(8,128)(2,1)S(1)} %convolution_convert_fusion.3), channel_id=1, replica_groups=mesh['seq'=32,'head'=8,'doc'=2] {'seq'}, dimensions={0}, use_global_device_ids=true | all-gather | bytes 540672 | tf_op jit(solution)/shard_map/all_gather | solution.py:110
  154.7 48.0 %all_gather.25 = bf16[2048,128]{1,0:T(8,128)(2,1)S(1)} all-gather(bf16[64,128]{1,0:T(8,128)(2,1)S(1)} %convolution_convert_fusion.2), channel_id=1, replica_groups=mesh['seq'=32,'head'=8,'doc'=2] {'seq'}, dimensions={0}, use_global_device_ids=true | all-gather | bytes 540672 | tf_op jit(solution)/shard_map/all_gather | solution.py:68
  203.1 47.6 %all_gather.26 = bf16[2048,128]{1,0:T(8,128)(2,1)S(1)} all-gather(bf16[64,128]{1,0:T(8,128)(2,1)S(1)} %convolution_convert_fusion.1), channel_id=1, replica_groups=mesh['seq'=32,'head'=8,'doc'=2] {'seq'}, dimensions={0}, use_global_device_ids=true | all-gather | bytes 540672 | tf_op jit(solution)/shard_map/all_gather | solution.py:69
  252.2 48.0 %all_gather.29 = bf16[2048,128]{1,0:T(8,128)(2,1)S(1)} all-gather(bf16[64,128]{1,0:T(8,128)(2,1)S(1)} %get-tuple-element.8), channel_id=1, replica_groups=mesh['seq'=32,'head'=8,'doc'=2] {'seq'}, dimensions={0}, use_global_device_ids=true | all-gather | bytes 540672 | tf_op jit(solution)/shard_map/all_gather | solution.py:113
  300.2 1.7 fusion.19
  302.1 1.8 fusion.56
  304.0 126.1 %all-reduce.3 = (f32[2048]{0:T(1024)S(1)}, f32[2048]{0:T(1024)S(1)}) all-reduce(f32[2048]{0:T(1024)S(1)} %get-tuple-element.5, f32[2048]{0:T(1024)S(1)} %dynamic-update-slice.2), channel_id=2, replica_groups=mesh['seq'=32,'head'=8,'doc'=2] {'seq'}, use_global_device_ids=true, to_apply=%add.1 | all-reduce | flops 4096 | bytes 32768
  430.1 2.2 fusion.5
  432.3 1.5 fusion.18
  435.0 2.1 fusion.13
  437.2 90.4 %all-reduce.6.cloned.1.call-done = bf16[64,1024]{1,0:T(8,128)(2,1)} async-done(((bf16[64,1024]{1,0:T(8,128)(2,1)}), bf16[64,1024]{1,0:T(8,128)(2,1)}) %all-reduce.6.cloned.1.call-update) | async-done | bytes 131088 | tf_op jit(solution)/shard_map/psum | solution.py:178
  528.7 1.7 fusion.39
  530.3 2.6 scatter_custom_fusion
  533.7 3.5 collective-permute-start.1
  537.2 1.8 constant_dynamic-update-slice_fusion.1
  539.1 2.5 collective-permute-done.1
  541.6 2.2 fusion.8
  543.9 4.2 scatter_custom_fusion.1
  548.1 2.7 convert_element_type.113
  (71 shorter events, 18.7 us)
Async XLA Ops:
  7.2 84.1 %copy-start = (bf16[1024,1024]{1,0:T(8,128)(2,1)S(1)}, bf16[1024,1024]{1,0:T(8,128)(2,1)}, u32[]{:S(2)}) copy-start(bf16[1024,1024]{1,0:T(8,128)(2,1)} %param.14) | copy-start | bytes 6291460
  7.2 520.4 %all-reduce.6.cloned.1.call-start = ((), (), s32[]{:S(2)}) async-start(), calls=%async_computation | async-start | bytes 262144 | tf_op jit(solution)/shard_map/psum | solution.py:178
  8.1 76.2 %collective-permute-start = (bf16[3,1024]{1,0:T(4,128)(2,1)S(1)}, bf16[3,1024]{1,0:T(4,128)(2,1)S(1)}, u32[]{:S(2)}, u32[]{:S(2)}) collective-permute-start(bf16[3,1024]{1,0:T(4,128)(2,1)S(1)} %slice.68), channel_id=1, source_target_pairs={{0,16},{16,32},{32,48},{48,64},{64,80},{80,96},{96,112},{112,128},... | collective-permute-start | bytes 18440 | tf_op jit(solution)/shard_map/ppermute | solution.py:16
  11.4 70.2 %copy-start.15 = (s32[64]{0:T(128)}, s32[64]{0:T(128)S(1)}, u32[]{:S(2)}) copy-start(s32[64]{0:T(128)S(1)} %get-tuple-element.29) | copy-start | bytes 772
  89.9 3.4 copy-start.9
  91.2 2.1 copy-start.8
  91.2 2.3 copy-start.6
  91.2 2.5 copy-start.7
  93.2 109.5 %copy-start.12 = (pred[2048]{0:T(1024)(128)(4,1)S(1)}, pred[2048]{0:T(1024)(128)(4,1)}, u32[]{:S(2)}) copy-start(pred[2048]{0:T(1024)(128)(4,1)} %broadcast_compare_fusion) | copy-start | bytes 6148
  93.2 109.5 %copy-start.14 = (s32[64]{0:T(128)S(1)}, s32[64]{0:T(128)}, u32[]{:S(2)}) copy-start(s32[64]{0:T(128)} %iota_add_fusion) | copy-start | bytes 772
  93.5 157.6 %copy-start.11 = (bf16[64,128]{1,0:T(8,128)(2,1)S(1)}, bf16[64,128]{1,0:T(8,128)(2,1)}, u32[]{:S(2)}) copy-start(bf16[64,128]{1,0:T(8,128)(2,1)} %param.21) | copy-start | bytes 49156
  93.5 157.6 %copy-start.13 = (pred[64]{0:T(512)(128)(4,1)S(1)}, pred[64]{0:T(512)(128)(4,1)}, u32[]{:S(2)}) copy-start(pred[64]{0:T(512)(128)(4,1)} %iota_compare_fusion.2) | copy-start | bytes 196
  202.7 49.4 %copy-start.2 = (bf16[2048,128]{1,0:T(8,128)(2,1)}, bf16[2048,128]{1,0:T(8,128)(2,1)S(1)}, u32[]{:S(2)}) copy-start(bf16[2048,128]{1,0:T(8,128)(2,1)S(1)} %all_gather.25) | copy-start | bytes 1572868
  250.7 1.4 copy-start.3
  301.8 130.4 %copy-start.4 = (bf16[2048,128]{1,0:T(8,128)(2,1)S(1)}, bf16[2048,128]{1,0:T(8,128)(2,1)}, u32[]{:S(2)}) copy-start(bf16[2048,128]{1,0:T(8,128)(2,1)} %all_gather.27) | copy-start | bytes 1572868
  533.7 7.9 %copy-start.1 = (f32[512,1024]{1,0:T(8,128)S(1)}, f32[512,1024]{1,0:T(8,128)}, u32[]{:S(2)}) copy-start(f32[512,1024]{1,0:T(8,128)} %scatter_custom_fusion) | copy-start | bytes 6291460
  533.7 7.9 %copy-start.10 = (f32[1,1024]{1,0:T(1,128)S(1)}, f32[1,1024]{1,0:T(1,128)}, u32[]{:S(2)}) copy-start(f32[1,1024]{1,0:T(1,128)} %get-tuple-element.18) | copy-start | bytes 12292
  533.7 7.9 %collective-permute-start.1 = (f32[3,1024]{1,0:T(4,128)S(1)}, f32[3,1024]{1,0:T(4,128)S(1)}, u32[]{:S(2)}, u32[]{:S(2)}) collective-permute-start(f32[3,1024]{1,0:T(4,128)S(1)} %slice.50), channel_id=1, source_target_pairs={{16,0},{32,16},{48,32},{64,48},{80,64},{96,80},{112,96},{128,112},... | collective-permute-start | bytes 36872 | tf_op jit(solution)/shard_map/ppermute | solution.py:16
  541.6 2.2 copy-start.5
Sparse Core Ops, SparseCore 0:
  437.3 90.2 all-reduce.5
where the time goes:
time: 559 us; the launch traced here: 558 us
  blocking collectives  394 us (70%)
  waiting for transfers between devices  93 us (17%)
  other arithmetic  18.4 us (3%)
  matrix products  16.1 us (3%)
  between operations  15.6 us (3%)
  local copies, waits for them, and re-layouts  14.4 us (3%)
  starting transfers between devices  6.1 us (1%)
    unnamed x2, blocking collectives  190 us
    psum x1, waiting for transfers between devices, per_device(): lax.psum(partial_normed.astype(jnp.bfloat16), 'head').astype(jnp.float32)  90.4 us
    all_gather x1, blocking collectives, per_device(): piece_queries = lax.all_gather(queries, 'seq', axis=0, tiled=True)  60.8 us
    all_gather x1, blocking collectives, per_device(): piece_grads = lax.all_gather(grad_rows, 'seq', axis=0, tiled=True)  48 us
    all_gather x1, blocking collectives, per_device(): piece_keys = lax.all_gather(key_rows, 'seq', axis=0, tiled=True)  48 us
    all_gather x1, blocking collectives, per_device(): piece_values = lax.all_gather(value_rows, 'seq', axis=0, tiled=True)  47.6 us
  transfers between devices with their start and end apart: 3, of which 2 were waited for; matrix products, arithmetic and copies ran while one was open for 2% of the time, Pallas kernels for 0%

commit v1 on v0

--- a/solution.py
+++ b/solution.py
@@ -175,7 +175,9 @@
     partial_normed = partial_normed + lax.dot_general(
         value_grad_rows, value_weight, contract, preferred_element_type=jnp.float32
     )
-    grad_normed = lax.psum(partial_normed.astype(jnp.bfloat16), "head").astype(jnp.float32)
+    grad_normed = jnp.sum(
+        lax.all_gather(partial_normed.astype(jnp.bfloat16), "head"), axis=0
+    ).astype(jnp.float32)
     scaled_grad = norm_gain * grad_normed
     cubed = inverse_rms * inverse_rms * inverse_rms
     grad_state = (

time: 559 us -> 523 us (0.936)
  waiting for transfers between devices: 93 us -> 57.3 us
    psum x1 -> x0, waiting for transfers between devices: 90.4 us -> none  [per_device(): lax.psum(partial_normed.astype(jnp.bfloat16), 'head').astype(jnp.float32)]
    all_gather x0 -> x1, waiting for transfers between devices: none -> 54.7 us  [per_device(): lax.all_gather(partial_normed.astype(jnp.bfloat16), 'head')]
where the time goes in v1:
time: 523 us; the launch traced here: 522 us
  blocking collectives  394 us (75%)
  waiting for transfers between devices  57.3 us (11%)
  other arithmetic  19.1 us (4%)
  between operations  15.6 us (3%)
  matrix products  15.2 us (3%)
  local copies, waits for them, and re-layouts  14.4 us (3%)
  starting transfers between devices  6.09 us (1%)
    unnamed x2, blocking collectives  190 us
    all_gather x1, blocking collectives, per_device(): piece_queries = lax.all_gather(queries, 'seq', axis=0, tiled=True)  60.8 us
    all_gather x1, waiting for transfers between devices, per_device(): lax.all_gather(partial_normed.astype(jnp.bfloat16), 'head')  54.7 us
    all_gather x1, blocking collectives, per_device(): piece_grads = lax.all_gather(grad_rows, 'seq', axis=0, tiled=True)  48 us
    all_gather x1, blocking collectives, per_device(): piece_keys = lax.all_gather(key_rows, 'seq', axis=0, tiled=True)  48 us
    all_gather x1, blocking collectives, per_device(): piece_values = lax.all_gather(value_rows, 'seq', axis=0, tiled=True)  47.6 us
  transfers between devices with their start and end apart: 3, of which 2 were waited for; matrix products, arithmetic and copies ran while one was open for 2% of the time, Pallas kernels for 0%

profile of v1, /device:TPU:56, one launch (start us, length us, event | category | flops | bytes accessed | tf_op | source)
XLA Modules:
  0.0 521.7 jit_solution(9210331461955616173)
XLA Ops:
  8.1 2.6 collective-permute-start
  16.0 63.5 %all-reduce = bf16[2048]{0:T(1024)(128)(2,1)S(1)} all-reduce(bf16[2048]{0:T(1024)(128)(2,1)S(1)} %dynamic-update-slice), channel_id=1, replica_groups=mesh['seq'=32,'head'=8,'doc'=2] {'seq'}, use_global_device_ids=true, to_apply=%add | all-reduce | flops 2048 | bytes 8192
  80.2 1.5 fusion.54
  82.2 2.2 gather_fusion
  84.4 1.5 pad_maximum_fusion
  91.4 1.9 multiply_reduce_fusion.1
  94.0 60.8 %all_gather.33 = bf16[2048,128]{1,0:T(8,128)(2,1)} all-gather(bf16[64,128]{1,0:T(8,128)(2,1)S(1)} %convolution_convert_fusion.3), channel_id=1, replica_groups=mesh['seq'=32,'head'=8,'doc'=2] {'seq'}, dimensions={0}, use_global_device_ids=true | all-gather | bytes 540672 | tf_op jit(solution)/shard_map/all_gather | solution.py:110
  154.8 48.0 %all_gather.31 = bf16[2048,128]{1,0:T(8,128)(2,1)S(1)} all-gather(bf16[64,128]{1,0:T(8,128)(2,1)S(1)} %convolution_convert_fusion.2), channel_id=1, replica_groups=mesh['seq'=32,'head'=8,'doc'=2] {'seq'}, dimensions={0}, use_global_device_ids=true | all-gather | bytes 540672 | tf_op jit(solution)/shard_map/all_gather | solution.py:68
  203.2 47.6 %all_gather.32 = bf16[2048,128]{1,0:T(8,128)(2,1)S(1)} all-gather(bf16[64,128]{1,0:T(8,128)(2,1)S(1)} %convolution_convert_fusion.1), channel_id=1, replica_groups=mesh['seq'=32,'head'=8,'doc'=2] {'seq'}, dimensions={0}, use_global_device_ids=true | all-gather | bytes 540672 | tf_op jit(solution)/shard_map/all_gather | solution.py:69
  252.3 48.0 %all_gather.35 = bf16[2048,128]{1,0:T(8,128)(2,1)S(1)} all-gather(bf16[64,128]{1,0:T(8,128)(2,1)S(1)} %get-tuple-element.8), channel_id=1, replica_groups=mesh['seq'=32,'head'=8,'doc'=2] {'seq'}, dimensions={0}, use_global_device_ids=true | all-gather | bytes 540672 | tf_op jit(solution)/shard_map/all_gather | solution.py:113
  300.3 1.7 fusion.19
  302.2 1.8 fusion.56
  304.1 126.1 %all-reduce.3 = (f32[2048]{0:T(1024)S(1)}, f32[2048]{0:T(1024)S(1)}) all-reduce(f32[2048]{0:T(1024)S(1)} %get-tuple-element.5, f32[2048]{0:T(1024)S(1)} %dynamic-update-slice.2), channel_id=2, replica_groups=mesh['seq'=32,'head'=8,'doc'=2] {'seq'}, use_global_device_ids=true, to_apply=%add.1 | all-reduce | flops 4096 | bytes 32768
  430.2 2.2 fusion.5
  432.4 1.5 fusion.18
  435.1 2.1 fusion.13
  437.2 54.7 %all-gather.5.cloned.1.call-done = bf16[512,1024]{1,0:T(8,128)(2,1)} async-done(((bf16[64,1024]{1,0:T(8,128)(2,1)}), bf16[512,1024]{1,0:T(8,128)(2,1)}) %all-gather.5.cloned.1.call-update) | async-done | bytes 1048592 | tf_op jit(solution)/shard_map/all_gather | solution.py:179
  494.3 2.7 scatter_custom_fusion
  497.7 3.5 collective-permute-start.1
  501.2 1.8 constant_dynamic-update-slice_fusion.1
  503.0 2.6 collective-permute-done.1
  505.6 2.2 fusion.8
  507.8 4.2 scatter_custom_fusion.1
  512.1 2.7 convert_element_type.115
  (70 shorter events, 18.6 us)
Async XLA Ops:
  7.2 84.2 %copy-start = (bf16[1024,1024]{1,0:T(8,128)(2,1)S(1)}, bf16[1024,1024]{1,0:T(8,128)(2,1)}, u32[]{:S(2)}) copy-start(bf16[1024,1024]{1,0:T(8,128)(2,1)} %param.14) | copy-start | bytes 6291460
  7.2 484.8 %all-gather.5.cloned.1.call-start = ((), (), s32[]{:S(2)}) async-start(), calls=%async_computation | async-start | bytes 1179648 | tf_op jit(solution)/shard_map/all_gather | solution.py:179
  8.1 76.3 %collective-permute-start = (bf16[3,1024]{1,0:T(4,128)(2,1)S(1)}, bf16[3,1024]{1,0:T(4,128)(2,1)S(1)}, u32[]{:S(2)}, u32[]{:S(2)}) collective-permute-start(bf16[3,1024]{1,0:T(4,128)(2,1)S(1)} %slice.68), channel_id=1, source_target_pairs={{0,16},{16,32},{32,48},{48,64},{64,80},{80,96},{96,112},{112,128},... | collective-permute-start | bytes 18440 | tf_op jit(solution)/shard_map/ppermute | solution.py:16
  11.4 70.3 %copy-start.14 = (s32[64]{0:T(128)}, s32[64]{0:T(128)S(1)}, u32[]{:S(2)}) copy-start(s32[64]{0:T(128)S(1)} %get-tuple-element.29) | copy-start | bytes 772
  90.0 3.3 copy-start.8
  91.3 2.1 copy-start.7
  91.3 2.3 copy-start.5
  91.3 2.5 copy-start.6
  93.3 109.5 %copy-start.11 = (pred[2048]{0:T(1024)(128)(4,1)S(1)}, pred[2048]{0:T(1024)(128)(4,1)}, u32[]{:S(2)}) copy-start(pred[2048]{0:T(1024)(128)(4,1)} %broadcast_compare_fusion) | copy-start | bytes 6148
  93.3 109.5 %copy-start.13 = (s32[64]{0:T(128)S(1)}, s32[64]{0:T(128)}, u32[]{:S(2)}) copy-start(s32[64]{0:T(128)} %iota_add_fusion) | copy-start | bytes 772
  93.6 157.6 %copy-start.10 = (bf16[64,128]{1,0:T(8,128)(2,1)S(1)}, bf16[64,128]{1,0:T(8,128)(2,1)}, u32[]{:S(2)}) copy-start(bf16[64,128]{1,0:T(8,128)(2,1)} %param.21) | copy-start | bytes 49156
  93.6 157.6 %copy-start.12 = (pred[64]{0:T(512)(128)(4,1)S(1)}, pred[64]{0:T(512)(128)(4,1)}, u32[]{:S(2)}) copy-start(pred[64]{0:T(512)(128)(4,1)} %iota_compare_fusion.2) | copy-start | bytes 196
  202.8 49.4 %copy-start.2 = (bf16[2048,128]{1,0:T(8,128)(2,1)}, bf16[2048,128]{1,0:T(8,128)(2,1)S(1)}, u32[]{:S(2)}) copy-start(bf16[2048,128]{1,0:T(8,128)(2,1)S(1)} %all_gather.31) | copy-start | bytes 1572868
  250.8 1.4 copy-start.3
  301.9 130.4 %copy-start.4 = (bf16[2048,128]{1,0:T(8,128)(2,1)S(1)}, bf16[2048,128]{1,0:T(8,128)(2,1)}, u32[]{:S(2)}) copy-start(bf16[2048,128]{1,0:T(8,128)(2,1)} %all_gather.33) | copy-start | bytes 1572868
  497.7 7.9 %copy-start.1 = (f32[512,1024]{1,0:T(8,128)S(1)}, f32[512,1024]{1,0:T(8,128)}, u32[]{:S(2)}) copy-start(f32[512,1024]{1,0:T(8,128)} %scatter_custom_fusion) | copy-start | bytes 6291460
  497.7 7.9 %copy-start.9 = (f32[1,1024]{1,0:T(1,128)S(1)}, f32[1,1024]{1,0:T(1,128)}, u32[]{:S(2)}) copy-start(f32[1,1024]{1,0:T(1,128)} %get-tuple-element.18) | copy-start | bytes 12292
  497.7 7.9 %collective-permute-start.1 = (f32[3,1024]{1,0:T(4,128)S(1)}, f32[3,1024]{1,0:T(4,128)S(1)}, u32[]{:S(2)}, u32[]{:S(2)}) collective-permute-start(f32[3,1024]{1,0:T(4,128)S(1)} %slice.50), channel_id=1, source_target_pairs={{16,0},{32,16},{48,32},{64,48},{80,64},{96,80},{112,96},{128,112},... | collective-permute-start | bytes 36872 | tf_op jit(solution)/shard_map/ppermute | solution.py:16
Sparse Core Ops, SparseCore 0:
  437.4 54.5 all-gather.4
